TPU v7x, 32 devices: a whole 2x2x4 slice. The times are simulated.
32 devices in a mesh: row: 4 (over z), col: 8 (over y, x, core).
Axes of the slice: x: 2, y: 2, z: 4, core: 2. Of those that a mesh axis runs over, the one named last changes fastest.
Arguments:
- covariance: float32 [8192, 8192], P('row', 'col'), as said below
- self_block: bfloat16 [8192, 512], P(('row', 'col')), may hold values from -0.25 to 0.25
- wake_block: bfloat16 [16, 4, 128, 128], replicated, may hold values from -0.375 to 0.375
- upstream: int32 [16, 4], replicated, may hold values from -1 to 15, as said below
- process_noise: float32 [8192], P('col'), may hold values from 0.5 to 2
- sensor_turbine: int32 [384], replicated, may hold values from 0 to 15
- azimuth_index: int32 [16], replicated, may hold values from 0 to 71
- sensor_weight: float32 [384, 512], replicated, may hold values from -0.25 to 0.25
- sensor_noise: float32 [384], replicated, may hold values from 0.5 to 2
Outputs:
- posterior: float32 [8192, 8192], P('row', 'col')
- kalman_gain: float32 [8192, 384], P('row', 'col')
Inputs may be any that keep to these rules, and one draw needn't show every extreme that they name: Row t lists distinct turbines other than t that lie upstream of t, valid entries first, then -1; some turbine lists 4. `covariance`: symmetric and positive definite.
All inputs are finite; a program needn't handle non-finite values.
Results may differ from a plain program's by a relative error of at most 0.0048.
Values may be sent and summed in bfloat16 or wider, within the bound.
No kernel may reach another device: no remote copies, remote signals or barrier semaphores. Data moves between devices by JAX's collectives and lax.ppermute only.
A program may use at most 128 MiB of HBM per device.

v0:
```python
import math
import jax
import jax.numpy as jnp
from jax import lax
from jax.sharding import PartitionSpec as P

TURB = 16
SPT = 512
INF = 128
NUP = 4
NAZ = 72


def broadcast(value, axis, root):
    mine = lax.axis_index(axis) == root
    return lax.psum(jnp.where(mine, value, jnp.zeros_like(value)), axis)


def observe_columns(sensor_weight, sensor_turbine, azimuth_index, start, count):
    sensors = sensor_weight.shape[0]
    matches = sensor_turbine[:, None] == jnp.arange(TURB)[None, :]
    rotor_index = jnp.sum(jnp.where(matches, azimuth_index[None, :], 0), axis=1)
    sensor_index = jnp.arange(sensors)
    blade_angle = rotor_index.astype(jnp.float32) * jnp.float32(2.0 * math.pi / NAZ) + (
        sensor_index % 3
    ).astype(jnp.float32) * jnp.float32(2.0 * math.pi / 3.0)
    positions = start + jnp.arange(count)
    turbine_of = positions // SPT
    offset_of = positions % SPT
    widened = jnp.tile(sensor_weight, (1, max(1, count // SPT)))
    weights = lax.dynamic_slice_in_dim(widened, start % SPT, count, 1)
    cosine = jnp.cos(blade_angle)[:, None]
    sine = jnp.sin(blade_angle)[:, None]
    factor = jnp.where(
        offset_of[None, :] < 2 * INF,
        jnp.float32(1.0),
        jnp.where(offset_of[None, :] < 3 * INF, cosine, sine),
    )
    return jnp.where(
        sensor_turbine[:, None] == turbine_of[None, :], weights * factor, jnp.float32(0.0)
    )


def split_bf16(x):
    high = x.astype(jnp.bfloat16)
    low = (x - high.astype(jnp.float32)).astype(jnp.bfloat16)
    return (high, low)


def coupling_matrix(wake_block, upstream, turbine):
    slots = upstream[turbine]
    blocks = jnp.zeros((INF, TURB, INF), jnp.bfloat16)
    for slot_index in range(NUP):
        anchor = slots[slot_index]
        hit = (jnp.arange(TURB) == anchor)[None, :, None]
        blocks = blocks + jnp.where(
            hit, wake_block[turbine, slot_index][:, None, :], jnp.zeros((), jnp.bfloat16)
        )
    return blocks.reshape(INF, TURB * INF)


def dot_f32(a, b, dims):
    return lax.dot_general(a, b, (dims, ((), ())), preferred_element_type=jnp.float32)


def shards(
    covariance,
    self_block,
    wake_block,
    upstream,
    process_noise,
    sensor_turbine,
    azimuth_index,
    sensor_weight,
    sensor_noise,
):
    row_count, col_count = covariance.shape
    row_start = lax.axis_index("row") * row_count
    col_start = lax.axis_index("col") * col_count
    per_row = row_count // SPT
    per_col = max(1, col_count // SPT)
    first_turbine = lax.axis_index("row") * per_row
    cov3 = covariance.reshape(per_row, SPT, col_count)
    inflow_all = lax.all_gather(cov3[:, :INF, :], "row", axis=0, tiled=True)
    inflow_high, inflow_low = split_bf16(inflow_all.reshape(TURB * INF, col_count))
    own_rows = lax.all_gather(self_block, "col", axis=0, tiled=True)
    cov_high, cov_low = split_bf16(cov3)
    blocks = []
    for local in range(per_row):
        turbine = first_turbine + local
        diag_rows = own_rows[local * SPT : (local + 1) * SPT]
        result = dot_f32(diag_rows, cov_high[local], ((1,), (0,))) + dot_f32(
            diag_rows, cov_low[local], ((1,), (0,))
        )
        coupling = coupling_matrix(wake_block, upstream, turbine)
        inflow_sum = dot_f32(coupling, inflow_high, ((1,), (0,))) + dot_f32(
            coupling, inflow_low, ((1,), (0,))
        )
        result = jnp.concatenate([result[:INF] + inflow_sum, result[INF:]], 0)
        blocks.append(result.astype(jnp.bfloat16))
    half_product = jnp.concatenate(blocks, 0)
    if col_count >= SPT:
        half3 = half_product.reshape(row_count, per_col, SPT)
        half_inflow = jnp.transpose(half3[:, :, :INF], (1, 0, 2))
        half_inflow_all = lax.all_gather(half_inflow, "col", axis=0, tiled=True)
        turbine_cols = [half3[:, local, :] for local in range(per_col)]
    else:
        full = lax.all_gather(half_product, "col", axis=1, tiled=True)
        half_inflow_all = jnp.transpose(full.reshape(row_count, TURB, SPT)[:, :, :INF], (1, 0, 2))
        turbine_cols = [lax.dynamic_slice_in_dim(full, col_start // SPT * SPT, SPT, 1)]
    target_rows = lax.dynamic_slice_in_dim(own_rows, col_start % row_count, col_count, 0)
    target_rows = broadcast(target_rows, "row", col_start // row_count)
    piece_width = min(col_count, SPT)
    pieces = []
    for local in range(per_col):
        turbine = col_start // SPT + local
        diag_rows = target_rows[local * piece_width : (local + 1) * piece_width]
        result = dot_f32(turbine_cols[local], diag_rows, ((1,), (1,)))
        coupling = coupling_matrix(wake_block, upstream, turbine).reshape(INF, TURB, INF)
        inflow_sum = dot_f32(half_inflow_all, coupling, ((0, 2), (1, 2)))
        inflow_sum = jnp.where(col_start % SPT == 0, inflow_sum, jnp.float32(0.0))
        pieces.append(jnp.concatenate([result[:, :INF] + inflow_sum, result[:, INF:]], 1))
    predicted = jnp.concatenate(pieces, 1)
    row_ids = row_start + jnp.arange(row_count)
    col_ids = col_start + jnp.arange(col_count)
    predicted = predicted + jnp.where(
        row_ids[:, None] == col_ids[None, :], process_noise[None, :], jnp.float32(0.0)
    )
    col_observe = observe_columns(
        sensor_weight, sensor_turbine, azimuth_index, col_start, col_count
    )
    partial_cross = jnp.dot(predicted, col_observe.T, precision=lax.Precision.HIGHEST)
    cross_cov = lax.psum(partial_cross, "col")
    row_observe = observe_columns(
        sensor_weight, sensor_turbine, azimuth_index, row_start, row_count
    )
    partial_innovation = jnp.dot(row_observe, cross_cov, precision=lax.Precision.HIGHEST)
    innovation = lax.psum(partial_innovation, "row") + jnp.diag(sensor_noise)
    symmetric = 0.5 * (innovation + innovation.T)
    lower = jnp.linalg.cholesky(symmetric)
    sensors = symmetric.shape[0]
    lower_inverse = jax.scipy.linalg.solve_triangular(
        lower, jnp.eye(sensors, dtype=jnp.float32), lower=True
    )
    inverse = jnp.dot(lower_inverse.T, lower_inverse, precision=lax.Precision.HIGHEST)
    gain_block = jnp.dot(cross_cov, inverse, precision=lax.Precision.HIGHEST)
    target_cross = lax.dynamic_slice_in_dim(cross_cov, col_start % row_count, col_count, 0)
    target_cross = broadcast(target_cross, "row", col_start // row_count)
    posterior = predicted - jnp.dot(gain_block, target_cross.T, precision=lax.Precision.HIGHEST)
    share = gain_block.shape[1] // lax.axis_size("col")
    gain_share = lax.dynamic_slice_in_dim(gain_block, lax.axis_index("col") * share, share, 1)
    return (posterior, gain_share)


def solution(mesh):
    in_specs = (P("row", "col"), P(("row", "col"), None), P(), P(), P("col"), P(), P(), P(), P())
    out_specs = (P("row", "col"), P("row", "col"))
    return jax.shard_map(shards, mesh=mesh, in_specs=in_specs, out_specs=out_specs, check_vma=False)
```

profile of v0, /device:TPU:0, one launch (start us, length us, event | category | flops | bytes accessed | tf_op | source)
XLA Modules:
  0.0 682.4 jit_solution(16363561873510141729)
XLA Ops:
  8.0 3.1 slice.340
  32.1 11.9 %subtract_convert_fusion.1 = (bf16[4,512,1024]{2,1,0:T(8,128)(2,1)}, bf16[4,512,1024]{2,1,0:T(8,128)(2,1)}) fusion(f32[4,512,1024]{2,1,0:T(8,128)} %bitcast.250), kind=kLoop, calls=%fused_computation.4 | loop fusion | flops 8388608 | bytes 16777216 | tf_op jit(solution)/shard_map/convert_element_type | solution.py:46
  44.0 2.1 fusion.39
  46.1 2.3 bitcast_add_fusion.1
  62.0 129.8 %all-gather.6.cloned.1.call-done = f32[16,128,1024]{2,1,0:T(8,128)} async-done(((f32[4,128,1024]{2,1,0:T(8,128)}), f32[16,128,1024]{2,1,0:T(8,128)}) %all-gather.6.cloned.1.call-update) | async-done | bytes 8388624 | tf_op jit(solution)/shard_map/all_gather | solution.py:84
  191.8 8.7 %subtract_convert_fusion = (bf16[16,128,1024]{2,1,0:T(8,128)(2,1)S(1)}, bf16[16,128,1024]{2,1,0:T(8,128)(2,1)S(1)}) fusion(f32[16,128,1024]{2,1,0:T(8,128)} %all-gather.6.cloned.1.call-done), kind=kLoop, calls=%fused_computation.3 | loop fusion | flops 8388608 | bytes 16777216 | tf_op jit(solution)/shard_map/convert_element_type | solution.py:46
  212.3 2.0 copy-done.4
  223.4 20.8 %all-reduce.6.cloned.1.call-done = bf16[1024,512]{1,0:T(8,128)(2,1)} async-done(((bf16[1024,512]{1,0:T(8,128)(2,1)}), bf16[1024,512]{1,0:T(8,128)(2,1)}) %all-reduce.6.cloned.1.call-update) | async-done | bytes 1048592 | tf_op jit(solution)/shard_map/psum | solution.py:16
  244.2 3.0 fusion.10
  247.4 3.5 copy-done.5
  252.5 2.0 copy-done.1
  256.4 43.6 %all-gather.8.cloned.1.call-done = bf16[16,2048,128]{2,1,0:T(8,128)(2,1)} async-done(((bf16[2,2048,128]{2,1,0:T(8,128)(2,1)}), bf16[16,2048,128]{2,1,0:T(8,128)(2,1)}) %all-gather.8.cloned.1.call-update) | async-done | bytes 8388624 | tf_op jit(solution)/shard_map/all_gather | solution.py:105
  299.9 6.6 fusion.9
  306.6 4.5 fusion.8
  312.1 38.5 %fusion.17 = f32[2048,384]{1,0:T(8,128)} fusion(f32[384,1024]{1,0:T(8,128)S(1)} %bitcast.258, f32[384]{0:T(512)S(1)} %get-tuple-element.103, f32[384]{0:T(512)S(1)} %get-tuple-element.102, s32[1024]{0:T(1024)S(1)} %get-tuple-element.104, s32[384]{0:T(512)S(1)} %copy-done.33, pred[1024]{0:T(1024)(128)(4,1)S(1)} %get-tuple-element.106, ...), kind=kOutput, calls=%fused_computation.36 | convolution fusion | flops 9678225408 | bytes 13134336 | tf_op jit(solution)/shard_map/dot_general | solution.py:132
  353.8 66.4 %all-reduce.8.cloned.1.call-done = f32[2048,384]{1,0:T(8,128)} async-done(((f32[2048,384]{1,0:T(8,128)}), f32[2048,384]{1,0:T(8,128)}) %all-reduce.8.cloned.1.call-update) | async-done | bytes 3145744 | tf_op jit(solution)/shard_map/psum | solution.py:133
  420.2 2.7 dynamic-slice_select_fusion
  422.8 8.5 %fusion = f32[384,384]{0,1:T(8,128)} fusion(f32[2048,384]{1,0:T(8,128)} %all-reduce.8.cloned.1.call-done, f32[384,2048]{1,0:T(8,128)S(1)} %bitcast.253, f32[384]{0:T(512)S(1)} %get-tuple-element.103, f32[384]{0:T(512)S(1)} %get-tuple-element.102, s32[2048]{0:T(1024)S(1)} %add_select_fusion.1, s32[384]{0:T(512)S(1)} %copy-done.33, ...), kind=kOutput, calls=%fused_computation.6 | convolution fusion | flops 3627810816 | bytes 6898176 | tf_op jit(solution)/shard_map/dot_general | solution.py:137
  432.8 88.4 %all-reduce.10.cloned.1.call-done = (f32[384,384]{0,1:T(8,128)}, f32[1024,384]{1,0:T(8,128)}) async-done(((f32[384,384]{0,1:T(8,128)}, f32[1024,384]{1,0:T(8,128)}), (f32[384,384]{0,1:T(8,128)}, f32[1024,384]{1,0:T(8,128)})) %all-reduce.10.cloned.1.call-update) | async-done | bytes 2162704 | tf_op jit(solution)/shard_map/psum | solution.py:138
  524.0 11.8 %cholesky.76 = f32[128,128]{1,0:T(8,128)S(1)} custom-call(f32[128,128]{1,0:T(8,128)S(1)} %cholesky.189), custom_call_target="Cholesky" | custom-call | tf_op jit(solution)/shard_map/jit(cholesky)/cholesky | solution.py:140
  536.6 9.8 %custom-call.23 = f32[1,128,128]{1,2,0:T(8,128)S(1)} custom-call(f32[1,128,128]{2,1,0:T(8,128)S(1)} %get-tuple-element.71), custom_call_target="InvertDiagBlocksLowerTriangular" | custom-call | tf_op jit(solution)/shard_map/jit(cholesky)/cholesky | solution.py:140
  547.1 11.7 %cholesky.160 = f32[128,128]{1,0:T(8,128)S(1)} custom-call(f32[128,128]{1,0:T(8,128)S(1)} %cholesky.193), custom_call_target="Cholesky" | custom-call | tf_op jit(solution)/shard_map/jit(cholesky)/cholesky | solution.py:140
  560.1 10.4 %custom-call.24 = f32[1,128,128]{1,2,0:T(8,128)} custom-call(f32[1,128,128]{2,1,0:T(8,128)S(1)} %get-tuple-element.69), custom_call_target="InvertDiagBlocksLowerTriangular" | custom-call | tf_op jit(solution)/shard_map/jit(cholesky)/cholesky | solution.py:140
  574.8 11.9 %cholesky.179 = f32[128,128]{1,0:T(8,128)S(1)} custom-call(f32[128,128]{1,0:T(8,128)S(1)} %convolution_subtract_fusion.4), custom_call_target="Cholesky" | custom-call | tf_op jit(solution)/shard_map/jit(cholesky)/cholesky | solution.py:140
  595.3 11.1 %while.1 = (s32[]{:T(128)}, f32[384,384]{0,1:T(8,128)}, s32[3,2]{0,1:T(2,128)S(1)}, f32[3,128,128]{2,1,0:T(8,128)}, s32[]{:T(128)}) while((s32[]{:T(128)}, f32[384,384]{0,1:T(8,128)}, s32[3,2]{0,1:T(2,128)S(1)}, f32[3,128,128]{2,1,0:T(8,128)}, s32[]{:T(128)}) %tuple.95), condition=%wide.while_cond, body=%wide.while_body.sunk | while | flops 2 | bytes 393329 | solution.py:142
  596.0 2.3 dynamic-slice.7
  599.7 2.3 dynamic-slice.7
  603.4 2.3 dynamic-slice.7
  606.4 30.3 %custom-call.25 = f32[3,128,128]{1,2,0:T(8,128)S(1)} custom-call(f32[3,128,128]{2,1,0:T(8,128)} %get-tuple-element.9), custom_call_target="InvertDiagBlocksLowerTriangular" | custom-call | tf_op jit(solution)/shard_map/jit(_solve_triangular)/triangular_solve | solution.py:142
  642.8 5.4 fusion.158
  648.3 16.8 %convolution_subtract_fusion = f32[2048,1024]{0,1:T(8,128)} fusion(f32[2048,384]{0,1:T(8,128)S(1)} %fusion.158, f32[1024,384]{1,0:T(8,128)S(1)} %copy-done.36, f32[1024]{0:T(1024)S(1)} %copy-done.38, s32[1024]{0:T(1024)S(1)} %copy-done.32, s32[2048]{0:T(1024)S(1)} %copy-done.29, f32[2048,384]{0,1:T(8,128)S(1)} %copy-done.12, f32[2048,128]{0,1:T(8,128)S(1)} %copy-done.56, ...), kind=kOutput, calls=%fused_computation.5 | convolution fusion | flops 9678356480 | bytes 21512192 | tf_op jit(solution)/shard_map/dot_general | solution.py:149
  665.9 9.2 %copy.81 = f32[2048,1024]{1,0:T(8,128)} copy(f32[2048,1024]{0,1:T(8,128)} %convolution_subtract_fusion) | data formatting | bytes 16777216
  (245 shorter events, 91.9 us)
Async XLA Ops:
  7.2 36.8 %all-gather.4.cloned.1.call-start = ((), (), s32[]{:S(2)}) async-start(), calls=%async_computation | async-start | bytes 2359296 | tf_op jit(solution)/shard_map/all_gather | solution.py:86
  7.9 183.8 %all-gather.6.cloned.1.call-start = ((), (), s32[]{:S(2)}) async-start(), calls=%async_computation.1 | async-start | bytes 10485760 | tf_op jit(solution)/shard_map/all_gather | solution.py:84
  11.1 233.1 %all-reduce.6.cloned.1.call-start = ((), (), s32[]{:S(2)}) async-start(), calls=%async_computation.2 | async-start | bytes 2097152 | tf_op jit(solution)/shard_map/psum | solution.py:16
  46.1 6.2 copy-start.3
  61.7 238.3 %all-gather.8.cloned.1.call-start = ((), (), s32[]{:S(2)}) async-start(), calls=%async_computation.3 | async-start | bytes 9437184 | tf_op jit(solution)/shard_map/all_gather | solution.py:105
  191.8 8.8 %copy-start.24 = (bf16[128,128]{1,0:T(8,128)(2,1)S(1)}, bf16[128,128]{1,0:T(8,128)(2,1)}, u32[]{:S(2)}) copy-start(bf16[128,128]{1,0:T(8,128)(2,1)} %get-tuple-element.54) | copy-start | bytes 98308
  191.8 8.8 %copy-start.25 = (bf16[128,128]{1,0:T(8,128)(2,1)S(1)}, bf16[128,128]{1,0:T(8,128)(2,1)}, u32[]{:S(2)}) copy-start(bf16[128,128]{1,0:T(8,128)(2,1)} %get-tuple-element.55) | copy-start | bytes 98308
  191.8 8.8 %copy-start.26 = (bf16[128,128]{1,0:T(8,128)(2,1)S(1)}, bf16[128,128]{1,0:T(8,128)(2,1)}, u32[]{:S(2)}) copy-start(bf16[128,128]{1,0:T(8,128)(2,1)} %get-tuple-element.56) | copy-start | bytes 98308
  191.8 8.8 %copy-start.27 = (bf16[128,128]{1,0:T(8,128)(2,1)S(1)}, bf16[128,128]{1,0:T(8,128)(2,1)}, u32[]{:S(2)}) copy-start(bf16[128,128]{1,0:T(8,128)(2,1)} %get-tuple-element.57) | copy-start | bytes 98308
  214.3 8.9 %copy-start.33 = (s32[384]{0:T(512)S(1)}, s32[384]{0:T(512)}, u32[]{:S(2)}) copy-start(s32[384]{0:T(512)} %param.14) | copy-start | bytes 4612
  214.3 8.9 %copy-start.34 = (s32[16]{0:T(128)S(1)}, s32[16]{0:T(128)}, u32[]{:S(2)}) copy-start(s32[16]{0:T(128)} %param.15) | copy-start | bytes 196
  215.5 204.7 %all-reduce.8.cloned.1.call-start = ((), (), s32[]{:S(2)}) async-start(), calls=%async_computation.4 | async-start | bytes 6291456 | tf_op jit(solution)/shard_map/psum | solution.py:133
  223.2 87.9 %copy-start.31 = (s32[1024]{0:T(1024)}, s32[1024]{0:T(1024)S(1)}, u32[]{:S(2)}) copy-start(s32[1024]{0:T(1024)S(1)} %get-tuple-element.105) | copy-start | bytes 12292
  223.3 87.9 %copy-start.28 = (s32[2048]{0:T(1024)}, s32[2048]{0:T(1024)S(1)}, u32[]{:S(2)}) copy-start(s32[2048]{0:T(1024)S(1)} %iota_add_fusion) | copy-start | bytes 24580
  247.2 5.3 copy-start
  251.2 59.9 %copy-start.11 = (f32[2048,384]{0,1:T(8,128)}, f32[2048,384]{0,1:T(8,128)S(1)}, u32[]{:S(2)}) copy-start(f32[2048,384]{0,1:T(8,128)S(1)} %slice.365) | copy-start | bytes 9437188
  299.9 6.6 copy-start.35
  306.6 5.5 copy-start.13
  306.6 5.5 copy-start.21
  306.6 5.5 copy-start.37
  350.6 170.6 %all-reduce.10.cloned.1.call-start = ((), (), s32[]{:S(2)}) async-start(), calls=%async_computation.5 | async-start | bytes 4325376 | tf_op jit(solution)/shard_map/psum | solution.py:138
  422.8 98.4 %copy-start.30 = (f32[384]{0:T(512)S(1)}, f32[384]{0:T(512)}, u32[]{:S(2)}) copy-start(f32[384]{0:T(512)} %param.17) | copy-start | bytes 4612
  524.0 46.6 %copy-start.20 = (f32[384,384]{1,0:T(8,128)}, f32[384,384]{1,0:T(8,128)S(1)}, u32[]{:S(2)}) copy-start(f32[384,384]{1,0:T(8,128)S(1)} %fusion.56) | copy-start | bytes 1769476
  570.6 72.2 %copy-start.7 = (f32[2048,384]{1,0:T(8,128)S(1)}, f32[2048,384]{1,0:T(8,128)}, u32[]{:S(2)}) copy-start(f32[2048,384]{1,0:T(8,128)} %all-reduce.8.cloned.1.call-done) | copy-start | bytes 9437188
  637.0 11.1 %copy-start.56 = (f32[2048,128]{0,1:T(8,128)S(1)}, f32[2048,128]{0,1:T(8,128)}, u32[]{:S(2)}) copy-start(f32[2048,128]{0,1:T(8,128)} %copy-done.55) | copy-start | bytes 3145732
  639.0 9.2 %copy-start.54 = (f32[2048,128]{0,1:T(8,128)S(1)}, f32[2048,128]{0,1:T(8,128)}, u32[]{:S(2)}) copy-start(f32[2048,128]{0,1:T(8,128)} %copy-done.53) | copy-start | bytes 3145732
  640.9 7.3 %copy-start.12 = (f32[2048,384]{0,1:T(8,128)S(1)}, f32[2048,384]{0,1:T(8,128)}, u32[]{:S(2)}) copy-start(f32[2048,384]{0,1:T(8,128)} %copy-done.11) | copy-start | bytes 9437188
  640.9 7.3 %copy-start.14 = (f32[2048,384]{0,1:T(8,128)S(1)}, f32[2048,384]{0,1:T(8,128)}, u32[]{:S(2)}) copy-start(f32[2048,384]{0,1:T(8,128)} %slice.361) | copy-start | bytes 9437188
  640.9 7.3 %copy-start.29 = (s32[2048]{0:T(1024)S(1)}, s32[2048]{0:T(1024)}, u32[]{:S(2)}) copy-start(s32[2048]{0:T(1024)} %copy-done.28) | copy-start | bytes 24580
  640.9 7.3 %copy-start.32 = (s32[1024]{0:T(1024)S(1)}, s32[1024]{0:T(1024)}, u32[]{:S(2)}) copy-start(s32[1024]{0:T(1024)} %copy-done.31) | copy-start | bytes 12292
  640.9 7.3 %copy-start.36 = (f32[1024,384]{1,0:T(8,128)S(1)}, f32[1024,384]{1,0:T(8,128)}, u32[]{:S(2)}) copy-start(f32[1024,384]{1,0:T(8,128)} %get-tuple-element.37) | copy-start | bytes 4718596
  641.0 7.3 %copy-start.38 = (f32[1024]{0:T(1024)S(1)}, f32[1024]{0:T(1024)}, u32[]{:S(2)}) copy-start(f32[1024]{0:T(1024)} %param.13) | copy-start | bytes 12292
  (31 other events, 68.8 us)
Sparse Core Ops, SparseCore 0:
  9.9 30.5 all-gather.3
  42.1 149.6 all-gather.5
  194.1 50.0 all-reduce.5
  246.1 53.7 all-gather.7
  350.7 69.4 all-reduce.7
  431.5 89.6 all-reduce.9
where the time goes:
time: 690 us; the launch traced here: 682 us
  waiting for transfers between devices  350 us (51%)
  other arithmetic  144 us (21%)
  matrix products  112 us (16%)
  local copies, waits for them, and re-layouts  58.7 us (9%)
  between operations  17.8 us (3%)
    all_gather x1, waiting for transfers between devices, shards(): inflow_all = lax.all_gather(cov3[:, :INF, :], 'row', axis=0, tiled=True)  130 us
    psum x1, waiting for transfers between devices, shards(): innovation = lax.psum(partial_innovation, 'row') + jnp.diag(sensor_noise)  88.4 us
    psum x1, waiting for transfers between devices, shards(): cross_cov = lax.psum(partial_cross, 'col')  66.4 us
    another operation x11, other arithmetic, shards(): lower = jnp.linalg.cholesky(symmetric)  60.4 us
    all_gather x1, waiting for transfers between devices, shards(): half_inflow_all = lax.all_gather(half_inflow, 'col', axis=0, tiled=True)  43.6 us
    dot_general x1, matrix products, shards(): jnp.dot(predicted, col_observe.T, precision=lax.Precision.HIGHEST)  38.5 us
    dot_general x20, matrix products, dot_f32(): lax.dot_general(a, b, (dims, ((), ())), preferred_element_type=jnp.float32)  34.1 us
    another operation x3, other arithmetic, shards(): jax.scipy.linalg.solve_triangular(lower, jnp.eye(sensors, dtype=jnp.float...  32.7 us
  transfers between devices with their start and end apart: 6, of which 5 were waited for; matrix products, arithmetic and copies ran while one was open for 13% of the time, Pallas kernels for 0%

commit v1 on v0

--- a/solution.py
+++ b/solution.py
@@ -1,3 +1,4 @@
+import functools
 import math
 import jax
 import jax.numpy as jnp
@@ -9,6 +10,13 @@
 INF = 128
 NUP = 4
 NAZ = 72
+
+
+def perform_plane(local_array, axis_key):
+    return jnp.sum(lax.all_gather(local_array, axis_name=axis_key), 0)
+
+
+switch_halves_on_mesh = functools.partial(perform_plane, axis_key="row")
 
 
 def broadcast(value, axis, root):
@@ -135,7 +143,7 @@
         sensor_weight, sensor_turbine, azimuth_index, row_start, row_count
     )
     partial_innovation = jnp.dot(row_observe, cross_cov, precision=lax.Precision.HIGHEST)
-    innovation = lax.psum(partial_innovation, "row") + jnp.diag(sensor_noise)
+    innovation = switch_halves_on_mesh(partial_innovation) + jnp.diag(sensor_noise)
     symmetric = 0.5 * (innovation + innovation.T)
     lower = jnp.linalg.cholesky(symmetric)
     sensors = symmetric.shape[0]

time: 690 us -> 647 us (0.938)
  waiting for transfers between devices: 350 us -> 308 us
    psum x1 -> x0, waiting for transfers between devices: 88.4 us -> none  [shards(): innovation = lax.psum(partial_innovation, 'row') + jnp.diag(sensor_noise)]
    all_gather x0 -> x1, waiting for transfers between devices: none -> 48 us  [perform_plane(): return jnp.sum(lax.all_gather(local_array, axis_name=axis_key), 0)]
    dot_general x1, matrix products: 38.5 us -> 29.1 us  [shards(): jnp.dot(predicted, col_observe.T, precision=lax.Precision.HIGHEST)]
    unnamed x124 -> x114, local copies, waits for them, and re-layouts: 27.4 us -> 30.8 us
    psum x1 -> x2, waiting for transfers between devices: 20.8 us -> 20.8 us  [broadcast(): return lax.psum(jnp.where(mine, value, jnp.zeros_like(value)), axis)]
  transfers between devices with their start and end apart: 6 -> 7, of which waited for: 5 -> 5; matrix products, arithmetic and copies ran while one was open for 13% -> 34% of each run, Pallas kernels for 0% -> 0%
where the time goes in v1:
time: 647 us; the launch traced here: 640 us
  waiting for transfers between devices  308 us (48%)
  other arithmetic  143 us (22%)
  matrix products  110 us (17%)
  local copies, waits for them, and re-layouts  61.4 us (9%)
  between operations  17.3 us (3%)
    all_gather x1, waiting for transfers between devices, shards(): inflow_all = lax.all_gather(cov3[:, :INF, :], 'row', axis=0, tiled=True)  130 us
    psum x1, waiting for transfers between devices, shards(): cross_cov = lax.psum(partial_cross, 'col')  64.7 us
    another operation x11, other arithmetic, shards(): lower = jnp.linalg.cholesky(symmetric)  58.5 us
    all_gather x1, waiting for transfers between devices, perform_plane(): return jnp.sum(lax.all_gather(local_array, axis_name=axis_key), 0)  48 us
    all_gather x1, waiting for transfers between devices, shards(): half_inflow_all = lax.all_gather(half_inflow, 'col', axis=0, tiled=True)  43.5 us
    dot_general x20, matrix products, dot_f32(): lax.dot_general(a, b, (dims, ((), ())), preferred_element_type=jnp.float32)  34 us
    another operation x3, other arithmetic, shards(): jax.scipy.linalg.solve_triangular(lower, jnp.eye(sensors, dtype=jnp.float...  33.4 us
    unnamed x114, local copies, waits for them, and re-layouts  30.8 us
  transfers between devices with their start and end apart: 7, of which 5 were waited for; matrix products, arithmetic and copies ran while one was open for 34% of the time, Pallas kernels for 0%

profile of v1, /device:TPU:0, one launch (start us, length us, event | category | flops | bytes accessed | tf_op | source)
XLA Modules:
  0.0 639.5 jit_solution(11074762497728134798)
XLA Ops:
  8.0 3.2 slice.340
  32.1 11.9 %subtract_convert_fusion.1 = (bf16[4,512,1024]{2,1,0:T(8,128)(2,1)}, bf16[4,512,1024]{2,1,0:T(8,128)(2,1)}) fusion(f32[4,512,1024]{2,1,0:T(8,128)} %bitcast.246), kind=kLoop, calls=%fused_computation.4 | loop fusion | flops 8388608 | bytes 16777216 | tf_op jit(solution)/shard_map/convert_element_type | solution.py:54
  44.0 2.1 fusion.39
  46.2 2.3 bitcast_add_fusion.1
  61.9 129.9 %all-gather.8.cloned.1.call-done = f32[16,128,1024]{2,1,0:T(8,128)} async-done(((f32[4,128,1024]{2,1,0:T(8,128)}), f32[16,128,1024]{2,1,0:T(8,128)}) %all-gather.8.cloned.1.call-update) | async-done | bytes 8388624 | tf_op jit(solution)/shard_map/all_gather | solution.py:92
  191.8 8.6 %subtract_convert_fusion = (bf16[16,128,1024]{2,1,0:T(8,128)(2,1)S(1)}, bf16[16,128,1024]{2,1,0:T(8,128)(2,1)S(1)}) fusion(f32[16,128,1024]{2,1,0:T(8,128)} %all-gather.8.cloned.1.call-done), kind=kLoop, calls=%fused_computation.3 | loop fusion | flops 8388608 | bytes 16777216 | tf_op jit(solution)/shard_map/convert_element_type | solution.py:54
  223.5 20.8 %all-reduce.5.cloned.1.call-done = bf16[1024,512]{1,0:T(8,128)(2,1)} async-done(((bf16[1024,512]{1,0:T(8,128)(2,1)}), bf16[1024,512]{1,0:T(8,128)(2,1)}) %all-reduce.5.cloned.1.call-update) | async-done | bytes 1048592 | tf_op jit(solution)/shard_map/psum | solution.py:24
  244.3 3.0 fusion.10
  247.5 3.5 copy-done.5
  256.4 43.5 %all-gather.10.cloned.1.call-done = bf16[16,2048,128]{2,1,0:T(8,128)(2,1)} async-done(((bf16[2,2048,128]{2,1,0:T(8,128)(2,1)}), bf16[16,2048,128]{2,1,0:T(8,128)(2,1)}) %all-gather.10.cloned.1.call-update) | async-done | bytes 8388624 | tf_op jit(solution)/shard_map/all_gather | solution.py:113
  299.9 6.6 %fusion.9 = f32[2048,128]{0,1:T(8,128)S(1)} fusion(bf16[16,2048,128]{2,1,0:T(8,128)(2,1)} %all-gather.10.cloned.1.call-done, f32[2048,512]{0,1:T(8,128)} %copy-done.1, pred[16]{0:T(512)(128)(4,1)S(1)} %iota_compare_fusion.10, pred[16]{0:T(512)(128)(4,1)S(1)} %iota_compare_fusion.11, pred[16]{0:T(512)(128)(4,1)S(1)} %iota_compare_fusion.12, ...), kind=kOutput, calls=%fused_computation.17 | convolution fusion | flops 1076101120 | bytes 10616897 | tf_op jit(solution)/shard_map/dot_general | solution.py:71
  306.6 4.5 fusion.8
  312.1 29.1 %fusion.17 = f32[2048,384]{1,0:T(8,128)} fusion(f32[384,1024]{1,0:T(8,128)S(1)} %bitcast.256, f32[384]{0:T(512)S(1)} %get-tuple-element.92, f32[384]{0:T(512)S(1)} %get-tuple-element.91, s32[1024]{0:T(1024)S(1)} %get-tuple-element.95, s32[384]{0:T(512)S(1)} %copy-done.31, pred[1024]{0:T(1024)(128)(4,1)S(1)} %get-tuple-element.97, ...), kind=kOutput, calls=%fused_computation.36 | convolution fusion | flops 9678225408 | bytes 13134336 | tf_op jit(solution)/shard_map/dot_general | solution.py:140
  343.0 3.1 copy.70
  346.1 64.7 %all-reduce.7.cloned.1.call-done = f32[2048,384]{1,0:T(8,128)} async-done(((f32[2048,384]{1,0:T(8,128)}), f32[2048,384]{1,0:T(8,128)}) %all-reduce.7.cloned.1.call-update) | async-done | bytes 3145744 | tf_op jit(solution)/shard_map/psum | solution.py:141
  410.8 9.4 %fusion = f32[384,384]{1,0:T(8,128)} fusion(f32[2048,384]{1,0:T(8,128)} %all-reduce.7.cloned.1.call-done, f32[384,2048]{1,0:T(8,128)} %bitcast.250, f32[384]{0:T(512)S(1)} %get-tuple-element.92, f32[384]{0:T(512)S(1)} %get-tuple-element.91, s32[2048]{0:T(1024)S(1)} %add_select_fusion.1, s32[384]{0:T(512)S(1)} %copy-done.31, ...), kind=kOutput, calls=%fused_computation.6 | convolution fusion | flops 3627810816 | bytes 6898176 | tf_op jit(solution)/shard_map/dot_general | solution.py:145
  423.0 48.0 %all-gather.12.cloned.1.call-done = f32[1536,384]{1,0:T(8,128)} async-done(((f32[384,384]{1,0:T(8,128)}), f32[1536,384]{1,0:T(8,128)}) %all-gather.12.cloned.1.call-update) | async-done | bytes 2359312 | tf_op jit(solution)/shard_map/all_gather | solution.py:16
  470.9 2.7 reduce_sum.25
  473.6 2.1 copy.53
  477.9 11.7 %cholesky.76 = f32[128,128]{1,0:T(8,128)S(1)} custom-call(f32[128,128]{1,0:T(8,128)S(1)} %cholesky.189), custom_call_target="Cholesky" | custom-call | tf_op jit(solution)/shard_map/jit(cholesky)/cholesky | solution.py:148
  491.2 9.8 %custom-call.23 = f32[1,128,128]{1,2,0:T(8,128)S(1)} custom-call(f32[1,128,128]{2,1,0:T(8,128)S(1)} %get-tuple-element.60), custom_call_target="InvertDiagBlocksLowerTriangular" | custom-call | tf_op jit(solution)/shard_map/jit(cholesky)/cholesky | solution.py:148
  504.1 11.7 %cholesky.160 = f32[128,128]{1,0:T(8,128)S(1)} custom-call(f32[128,128]{1,0:T(8,128)S(1)} %cholesky.193), custom_call_target="Cholesky" | custom-call | tf_op jit(solution)/shard_map/jit(cholesky)/cholesky | solution.py:148
  517.1 10.2 %custom-call.24 = f32[1,128,128]{1,2,0:T(8,128)S(1)} custom-call(f32[1,128,128]{2,1,0:T(8,128)S(1)} %get-tuple-element.57), custom_call_target="InvertDiagBlocksLowerTriangular" | custom-call | tf_op jit(solution)/shard_map/jit(cholesky)/cholesky | solution.py:148
  529.4 11.7 %cholesky.179 = f32[128,128]{1,0:T(8,128)S(1)} custom-call(f32[128,128]{1,0:T(8,128)S(1)} %convolution_subtract_fusion.4), custom_call_target="Cholesky" | custom-call | tf_op jit(solution)/shard_map/jit(cholesky)/cholesky | solution.py:148
  546.9 10.6 %while.1 = (s32[]{:T(128)}, f32[384,384]{1,0:T(8,128)}, s32[3,2]{0,1:T(2,128)S(1)}, f32[3,128,128]{2,1,0:T(8,128)}, s32[]{:T(128)}) while((s32[]{:T(128)}, f32[384,384]{1,0:T(8,128)}, s32[3,2]{0,1:T(2,128)S(1)}, f32[3,128,128]{2,1,0:T(8,128)}, s32[]{:T(128)}) %tuple.95), condition=%wide.while_cond, body=%wide.while_body.sunk | while | flops 2 | bytes 132205 | solution.py:150
  547.5 2.9 bitcast_dynamic-update-slice_fusion.10
  551.1 2.9 bitcast_dynamic-update-slice_fusion.10
  554.6 2.8 bitcast_dynamic-update-slice_fusion.10
  557.4 30.9 %custom-call.25 = f32[3,128,128]{1,2,0:T(8,128)} custom-call(f32[3,128,128]{2,1,0:T(8,128)} %get-tuple-element.9), custom_call_target="InvertDiagBlocksLowerTriangular" | custom-call | tf_op jit(solution)/shard_map/jit(_solve_triangular)/triangular_solve | solution.py:150
  596.0 5.4 fusion.156
  603.9 19.4 %convolution_subtract_fusion = f32[2048,1024]{0,1:T(8,128)} fusion(f32[2048,384]{0,1:T(8,128)} %copy-done.8, f32[1024,384]{1,0:T(8,128)} %all-reduce.9.cloned.1.call-done, f32[1024]{0:T(1024)S(1)} %copy-done.35, s32[1024]{0:T(1024)S(1)} %copy-done.30, s32[2048]{0:T(1024)S(1)} %copy-done.28, f32[2048,384]{0,1:T(8,128)} %copy-done.12, ...), kind=kOutput, calls=%fused_computation.5 | convolution fusion | flops 9678356480 | bytes 21512192 | tf_op jit(solution)/shard_map/dot_general | solution.py:157
  623.2 9.2 %copy.55 = f32[2048,1024]{1,0:T(8,128)} copy(f32[2048,1024]{0,1:T(8,128)} %convolution_subtract_fusion) | data formatting | bytes 16777216
  (223 shorter events, 94.7 us)
Async XLA Ops:
  7.2 4.1 copy-start.21
  7.2 36.9 %all-gather.6.cloned.1.call-start = ((), (), s32[]{:S(2)}) async-start(), calls=%async_computation | async-start | bytes 2359296 | tf_op jit(solution)/shard_map/all_gather | solution.py:94
  7.9 183.8 %all-gather.8.cloned.1.call-start = ((), (), s32[]{:S(2)}) async-start(), calls=%async_computation.1 | async-start | bytes 10485760 | tf_op jit(solution)/shard_map/all_gather | solution.py:92
  11.1 233.1 %all-reduce.5.cloned.1.call-start = ((), (), s32[]{:S(2)}) async-start(), calls=%async_computation.2 | async-start | bytes 2097152 | tf_op jit(solution)/shard_map/psum | solution.py:24
  46.2 4.4 copy-start.6
  46.2 6.2 copy-start.3
  61.7 238.3 %all-gather.10.cloned.1.call-start = ((), (), s32[]{:S(2)}) async-start(), calls=%async_computation.3 | async-start | bytes 9437184 | tf_op jit(solution)/shard_map/all_gather | solution.py:113
  191.8 8.7 %copy-start.22 = (bf16[128,128]{1,0:T(8,128)(2,1)S(1)}, bf16[128,128]{1,0:T(8,128)(2,1)}, u32[]{:S(2)}) copy-start(bf16[128,128]{1,0:T(8,128)(2,1)} %get-tuple-element.40) | copy-start | bytes 98308
  191.8 8.7 %copy-start.23 = (bf16[128,128]{1,0:T(8,128)(2,1)S(1)}, bf16[128,128]{1,0:T(8,128)(2,1)}, u32[]{:S(2)}) copy-start(bf16[128,128]{1,0:T(8,128)(2,1)} %get-tuple-element.41) | copy-start | bytes 98308
  191.8 8.7 %copy-start.24 = (bf16[128,128]{1,0:T(8,128)(2,1)S(1)}, bf16[128,128]{1,0:T(8,128)(2,1)}, u32[]{:S(2)}) copy-start(bf16[128,128]{1,0:T(8,128)(2,1)} %get-tuple-element.42) | copy-start | bytes 98308
  191.8 8.7 %copy-start.25 = (bf16[128,128]{1,0:T(8,128)(2,1)S(1)}, bf16[128,128]{1,0:T(8,128)(2,1)}, u32[]{:S(2)}) copy-start(bf16[128,128]{1,0:T(8,128)(2,1)} %get-tuple-element.43) | copy-start | bytes 98308
  211.4 4.0 copy-start.17
  214.1 9.1 %copy-start.31 = (s32[384]{0:T(512)S(1)}, s32[384]{0:T(512)}, u32[]{:S(2)}) copy-start(s32[384]{0:T(512)} %param.14) | copy-start | bytes 4612
  214.2 9.1 %copy-start.32 = (s32[16]{0:T(128)S(1)}, s32[16]{0:T(128)}, u32[]{:S(2)}) copy-start(s32[16]{0:T(128)} %param.15) | copy-start | bytes 196
  215.3 195.5 %all-reduce.7.cloned.1.call-start = ((), (), s32[]{:S(2)}) async-start(), calls=%async_computation.4 | async-start | bytes 6291456 | tf_op jit(solution)/shard_map/psum | solution.py:141
  223.3 87.8 %copy-start.29 = (s32[1024]{0:T(1024)}, s32[1024]{0:T(1024)S(1)}, u32[]{:S(2)}) copy-start(s32[1024]{0:T(1024)S(1)} %get-tuple-element.96) | copy-start | bytes 12292
  223.3 87.8 %copy-start.27 = (s32[2048]{0:T(1024)}, s32[2048]{0:T(1024)S(1)}, u32[]{:S(2)}) copy-start(s32[2048]{0:T(1024)S(1)} %iota_add_fusion) | copy-start | bytes 24580
  247.2 5.3 copy-start
  247.2 4.0 copy-start.20
  251.2 59.9 %copy-start.12 = (f32[2048,384]{0,1:T(8,128)}, f32[2048,384]{0,1:T(8,128)S(1)}, u32[]{:S(2)}) copy-start(f32[2048,384]{0,1:T(8,128)S(1)} %slice.365) | copy-start | bytes 9437188
  299.9 6.6 %copy-start.33 = (bf16[16,2048,128]{2,1,0:T(8,128)(2,1)S(1)}, bf16[16,2048,128]{2,1,0:T(8,128)(2,1)}, u32[]{:S(2)}) copy-start(bf16[16,2048,128]{2,1,0:T(8,128)(2,1)} %all-gather.10.cloned.1.call-done) | copy-start | bytes 25165828
  306.6 4.6 copy-start.50
  306.6 5.6 copy-start.13
  306.6 5.6 copy-start.19
  306.6 5.5 copy-start.34
  341.2 129.7 %all-gather.12.cloned.1.call-start = ((), (), s32[]{:S(2)}) async-start(), calls=%async_computation.6 | async-start | bytes 2949120 | tf_op jit(solution)/shard_map/all_gather | solution.py:16
  410.8 10.9 %copy-start.7 = (f32[2048,384]{1,0:T(8,128)S(1)}, f32[2048,384]{1,0:T(8,128)}, u32[]{:S(2)}) copy-start(f32[2048,384]{1,0:T(8,128)} %all-reduce.7.cloned.1.call-done) | copy-start | bytes 9437188
  420.2 183.6 %all-reduce.9.cloned.1.call-start = ((), (), s32[]{:S(2)}) async-start(), calls=%async_computation.5 | async-start | bytes 3145728 | tf_op jit(solution)/shard_map/psum | solution.py:24
  421.7 54.0 %copy-start.26 = (f32[384]{0:T(512)S(1)}, f32[384]{0:T(512)}, u32[]{:S(2)}) copy-start(f32[384]{0:T(512)} %param.17) | copy-start | bytes 4612
  594.6 9.3 %copy-start.28 = (s32[2048]{0:T(1024)S(1)}, s32[2048]{0:T(1024)}, u32[]{:S(2)}) copy-start(s32[2048]{0:T(1024)} %copy-done.27) | copy-start | bytes 24580
  594.6 9.3 %copy-start.30 = (s32[1024]{0:T(1024)S(1)}, s32[1024]{0:T(1024)}, u32[]{:S(2)}) copy-start(s32[1024]{0:T(1024)} %copy-done.29) | copy-start | bytes 12292
  594.6 9.2 %copy-start.35 = (f32[1024]{0:T(1024)S(1)}, f32[1024]{0:T(1024)}, u32[]{:S(2)}) copy-start(f32[1024]{0:T(1024)} %param.13) | copy-start | bytes 12292
  (27 other events, 49.2 us)
Sparse Core Ops, SparseCore 0:
  9.9 30.5 all-gather.5
  42.1 149.6 all-gather.7
  194.1 50.0 all-reduce.4
  246.2 53.7 all-gather.9
  341.3 69.4 all-reduce.6
  420.4 50.5 all-gather.11
  473.3 68.0 all-reduce.8
